TPU v7x, 512 devices: a whole 4x8x8 slice. The times are simulated.
512 devices in a mesh: sub: 128 (over z, y, core), harm: 4 (over x).
Axes of the slice: x: 4, y: 8, z: 8, core: 2. Of those that a mesh axis runs over, the one named last changes fastest.
Arguments:
- lengths: int32 [384], P('sub'), may hold values from 128 to 1024, as said below
- owners: int32 [384, 1], P('sub'), may hold values from 0 to 127, as said below
- front_inverse: bfloat16 [384, 1024, 1024], P('sub', 'harm'), may hold values from -0.1875 to 0.1875
- coupling: bfloat16 [384, 1024, 768], P('sub', 'harm'), may hold values from -0.1875 to 0.1875
- stiffness: bfloat16 [384, 768, 768], P('sub', 'harm'), may hold values from -0.21875 to 0.21875
- displacement: bfloat16 [128, 32, 768], P('sub', 'harm'), may hold values from -6 to 6
- forcing: float32 [128, 32, 768], P('sub', 'harm'), may hold values from -6 to 6
- lumped_mass: float32 [128, 768], P('sub'), may hold values from 0.2 to 2
- damping: float32 [128, 768], P('sub'), may hold values from 0.1 to 1.5
Outputs:
- interior: bfloat16 [384, 32, 1024], P('sub', None, 'harm')
- residual: float32 [128, 32, 768], P('sub', 'harm')
- modes: bfloat16 [384, 1024, 768], P('sub', 'harm')
Inputs may be any that keep to these rules, and one draw needn't show every extreme that they name: `lengths`: live interior front rows of each substructure, which are its first rows; some substructure has all 1024. `owners`: substructure k lies on sub index k // 3; on every sub index d, the first 2 of its 3 substructures are attached to block (d + 64) mod 128, the third to a block of uneven popularity; every interface block has at least one substructure.
All inputs are finite; a program needn't handle non-finite values.
Results may differ from a plain program's by a relative error of at most 0.008.
Values may be sent and summed in bfloat16 or wider, within the bound.
No kernel may reach another device: no remote copies, remote signals or barrier semaphores. Data moves between devices by JAX's collectives and lax.ppermute only.
A program may use at most 64 MiB of HBM per device.

v0:
```python
import jax
import jax.numpy as jnp
from jax import lax
from jax.sharding import Mesh
from jax.sharding import PartitionSpec as P

SUB = ("sub_0", "sub_1", "sub_2")
PLANE = ("sub_0", "sub_1")
PAIR = ("sub_2", "harm")


def copy_for_each(x, axis):
    length = lax.axis_size(axis)
    return lax.all_to_all(jnp.broadcast_to(x[None], (length, *x.shape)), axis, 0, 0, tiled=True)


def joined_along(tiles, dim):
    tiles = jnp.moveaxis(tiles, 0, dim)
    shape = tiles.shape
    return tiles.reshape(*shape[:dim], shape[dim] * shape[dim + 1], *shape[dim + 2 :])


def whole_of(x, axes, dim):
    far, near = axes
    tiles = copy_for_each(copy_for_each(x, far), near)
    return joined_along(tiles.swapaxes(0, 1).reshape(-1, *x.shape), dim)


def collect(x, axis, dim):
    tiles = copy_for_each(x, axis)
    return joined_along(tiles, dim)


def in_blocks(x, dim, length):
    shape = x.shape
    tiles = x.reshape(*shape[:dim], length, shape[dim] // length, *shape[dim + 1 :])
    return jnp.moveaxis(tiles, dim, 0)


def sent_and_summed(x, axis, dim):
    tiles = in_blocks(x, dim, lax.axis_size(axis))
    arrived = lax.all_to_all(tiles, axis, split_axis=0, concat_axis=0, tiled=True)
    return arrived.astype(jnp.float32).sum(axis=0)


def body(
    lengths, owners, front_inverse, coupling, stiffness, displacement, forcing, lumped_mass, damping
):
    nharm = lax.axis_size("harm")
    harm_idx = lax.axis_index("harm")
    front_q = coupling.shape[1]
    width = coupling.shape[2]
    width_q = stiffness.shape[1]
    nown = lax.axis_size(SUB)
    own_rows = harm_idx * front_q + jnp.arange(front_q, dtype=jnp.int32)
    live_rows = own_rows[None, :] < lengths[:, None]
    masked = jnp.where(live_rows[:, :, None], coupling, jnp.zeros_like(coupling))
    piece = lax.all_gather(coupling, "harm", axis=1, tiled=True)
    live_cols = jnp.arange(nharm * front_q, dtype=jnp.int32)[None, :] < lengths[:, None]
    front_live = jnp.where(live_cols[:, None, :], front_inverse, jnp.zeros_like(front_inverse))
    modes = jnp.einsum(
        "sfg,sgn->sfn", front_live, piece, preferred_element_type=jnp.float32
    ).astype(jnp.bfloat16)
    nplane = lax.axis_size(PLANE)
    rows_q = displacement.shape[1]
    core = lax.axis_index("sub_2")
    near = (lax.axis_index(SUB) + nown // 2) % nown
    third = owners[2, 0]
    other = lax.ppermute(owners[2:3, 0], "sub_2", [(0, 1), (1, 0)])[0]
    plane = copy_for_each(displacement[0], PLANE)
    lent = lax.ppermute(
        lax.dynamic_index_in_dim(plane, other // 2, 0, keepdims=False), "sub_2", [(0, 1), (1, 0)]
    )
    here = lax.dynamic_index_in_dim(plane, third // 2, 0, keepdims=False)
    picked = jnp.stack(
        [
            lax.dynamic_index_in_dim(plane, near // 2, 0, keepdims=False),
            jnp.where(third % 2 == core, here, lent),
        ]
    )
    own_pair = collect(picked, "harm", 1)
    own_disp = jnp.stack([own_pair[0], own_pair[0], own_pair[1]])
    inner = -jnp.einsum("sfn,shn->shf", modes, own_disp, preferred_element_type=jnp.float32)
    interior = jnp.where(live_rows[:, None, :], inner, jnp.float32(0.0)).astype(jnp.bfloat16)
    disp_cols = lax.dynamic_slice_in_dim(own_disp, harm_idx * width_q, width_q, 2)
    contrib = jnp.einsum("shf,sfn->shn", interior, masked, preferred_element_type=jnp.float32)
    contrib = contrib + jnp.einsum(
        "shj,sjn->shn", disp_cols, stiffness, preferred_element_type=jnp.float32
    )
    near_c = (contrib[0] + contrib[1]).reshape(nharm, rows_q, width)
    third_c = contrib[2].reshape(nharm, rows_q, width)
    zero_rows = jnp.zeros_like(near_c)
    send = jnp.stack(
        [
            jnp.stack(
                [
                    jnp.where(peer_core == core, near_c, zero_rows),
                    jnp.where(third % 2 == peer_core, third_c, zero_rows),
                ],
                axis=1,
            )
            for peer_core in range(2)
        ]
    )
    came = lax.all_to_all(
        send.reshape(2 * nharm, 2, rows_q, width).astype(jnp.bfloat16), PAIR, 0, 0, tiled=True
    ).astype(jnp.float32)
    came = came.reshape(2, nharm, 2, rows_q, width).sum(axis=1)
    mine = jnp.where(core == 0, came[0], came[1])
    theirs = jnp.where(core == 0, came[1], came[0])
    near_part = mine[0]
    third_part = mine[1]
    other_part = theirs[1]
    slots = jnp.arange(nplane, dtype=jnp.int32)[:, None, None]
    dense = (
        jnp.where(slots == near // 2, near_part, jnp.float32(0.0))
        + jnp.where((slots == third // 2) & (third % 2 == core), third_part, jnp.float32(0.0))
        + jnp.where((slots == other // 2) & (other % 2 == core), other_part, jnp.float32(0.0))
    )
    arrived = lax.all_to_all(
        dense.astype(jnp.bfloat16), PLANE, split_axis=0, concat_axis=0, tiled=True
    ).astype(jnp.float32)
    gathered = jnp.sum(arrived, axis=0, keepdims=True)
    rows_q = displacement.shape[1]
    pairs_all = rows_q * nharm // 2
    rows = harm_idx * rows_q + jnp.arange(rows_q, dtype=jnp.int32)
    pair = (rows // 2).astype(jnp.float32)
    parity = (rows % 2).astype(jnp.float32)
    freq = 1.5 * (pair + 1.0) / pairs_all
    sign = 1.0 - 2.0 * parity
    disp = displacement.astype(jnp.float32)
    partner = disp.reshape(1, rows_q // 2, 2, width)[:, :, ::-1, :].reshape(1, rows_q, width)
    residual = (
        gathered
        - (freq * freq)[None, :, None] * lumped_mass[:, None, :] * disp
        + (sign * freq)[None, :, None] * damping[:, None, :] * partner
        - forcing
    )
    return (interior, residual, modes)


def solution(mesh):
    split = Mesh(
        mesh.devices.reshape(8, 8, 2, mesh.shape["harm"]), ("sub_0", "sub_1", "sub_2", "harm")
    )
    placed = (
        P(SUB),
        P(SUB, None),
        P(SUB, "harm", None),
        P(SUB, "harm", None),
        P(SUB, "harm", None),
        P(SUB, "harm", None),
        P(SUB, "harm", None),
        P(SUB, None),
        P(SUB, None),
    )
    return jax.shard_map(
        body,
        mesh=split,
        in_specs=placed,
        out_specs=(P(SUB, None, "harm"), P(SUB, "harm", None), P(SUB, "harm", None)),
        check_vma=False,
    )
```

profile of v0, /device:TPU:8, one launch (start us, length us, event | category | flops | bytes accessed | tf_op | source)
XLA Modules:
  0.0 136.1 jit_solution(10824814379573062923)
XLA Ops:
  7.2 0.0 copy-start
  7.2 0.0 all-gather.2.cloned.1.call-start
  7.2 0.7 all-gather.2.cloned.1.call-update
  7.9 1.6 %broadcast_in_dim.101 = bf16[64,8,768]{2,1,0:T(8,128)(2,1)} broadcast(bf16[8,768]{1,0:T(8,128)(2,1)} %bitcast.58), dimensions={1,2} | broadcast | bytes 798720 | tf_op jit(solution)/shard_map/broadcast_in_dim | solution.py:14
  9.6 16.6 %all-to-all-start = ((bf16[64,8,768]{2,1,0:T(8,128)(2,1)}), bf16[64,8,768]{2,1,0:T(8,128)(2,1)S(1)}, u32[]{:S(2)}, u32[]{:S(2)}) async-start(bf16[64,8,768]{2,1,0:T(8,128)(2,1)} %broadcast_in_dim.101), calls=%async_computation | async-start | bytes 1572864 | tf_op jit(solution)/shard_map/all_to_all | solution.py:14
  26.2 0.6 slice.46
  26.8 1.9 %collective-permute-start = (s32[1]{0:T(128)}, s32[1]{0:T(128)}, u32[]{:S(2)}, u32[]{:S(2)}) collective-permute-start(s32[1]{0:T(128)} %bitcast.3), channel_id=1, source_target_pairs={{0,4},{4,0},{1,5},{5,1},{2,6},{6,2},{3,7},{7,3},{8,12},{12,8},{9,1... | collective-permute-start | bytes 20 | tf_op jit(solution)/shard_map/ppermute | solution.py:69
  28.7 0.1 iota_compare_fusion
  28.8 1.1 collective-permute-done
  32.4 17.7 %all-to-all-done = bf16[64,8,768]{2,1,0:T(8,128)(2,1)S(1)} async-done(((bf16[64,8,768]{2,1,0:T(8,128)(2,1)}), bf16[64,8,768]{2,1,0:T(8,128)(2,1)S(1)}, u32[]{:S(2)}, u32[]{:S(2)}) %all-to-all-start) | async-done | bytes 786464 | tf_op jit(solution)/shard_map/all_to_all | solution.py:14
  50.1 1.9 %collective-permute-start.1 = (bf16[8,768]{1,0:T(8,128)(2,1)S(1)}, bf16[8,768]{1,0:T(8,128)(2,1)S(1)}, u32[]{:S(2)}, u32[]{:S(2)}) collective-permute-start(bf16[8,768]{1,0:T(8,128)(2,1)S(1)} %get-tuple-element.4), channel_id=1, source_target_pairs={{0,4},{4,0},{1,5},{5,1},{2,6},{6,2},{3,7},{7,3},{8,12},{12,8},{9,1... | collective-permute-start | bytes 36872 | tf_op jit(solution)/shard_map/ppermute | solution.py:71
  54.7 0.6 broadcast_in_dim.102
  55.4 4.3 %all-to-all-start.1 = ((bf16[4,2,8,768]{3,2,1,0:T(8,128)(2,1)}), bf16[4,2,8,768]{3,2,1,0:T(8,128)(2,1)S(1)}, u32[]{:S(2)}, u32[]{:S(2)}) async-start(bf16[4,2,8,768]{3,2,1,0:T(8,128)(2,1)} %broadcast_in_dim.102), calls=%async_computation.1 | async-start | bytes 196608 | tf_op jit(solution)/shard_map/all_to_all | solution.py:14
  59.7 0.1 broadcast_compare_fusion
  59.7 7.0 %all-to-all-done.1 = bf16[4,2,8,768]{3,2,1,0:T(8,128)(2,1)S(1)} async-done(((bf16[4,2,8,768]{3,2,1,0:T(8,128)(2,1)}), bf16[4,2,8,768]{3,2,1,0:T(8,128)(2,1)S(1)}, u32[]{:S(2)}, u32[]{:S(2)}) %all-to-all-start.1) | async-done | bytes 98336 | tf_op jit(solution)/shard_map/all_to_all | solution.py:14
  66.8 1.1 fusion.20
  67.9 5.9 %all-gather.2.cloned.1.call-done = bf16[3,1024,768]{2,1,0:T(8,128)(2,1)} async-done(((bf16[3,256,768]{2,1,0:T(8,128)(2,1)}), bf16[3,1024,768]{2,1,0:T(8,128)(2,1)}) %all-gather.2.cloned.1.call-update) | async-done | bytes 4718608 | tf_op jit(solution)/shard_map/all_gather | solution.py:58
  73.7 4.2 %fusion.3 = bf16[3,256,768]{2,1,0:T(8,128)(2,1)S(1)} fusion(bf16[3,1024,768]{2,1,0:T(8,128)(2,1)} %all-gather.2.cloned.1.call-done, bf16[3,256,1024]{2,1,0:T(8,128)(2,1)} %param.11, pred[3,1024]{1,0:T(4,128)(4,1)S(1)} %iota_compare_fusion), kind=kOutput, calls=%fused_computation.5 | convolution fusion | flops 1209335808 | bytes 7474176 | tf_op jit(solution)/shard_map/sfg,sgn->sfn/dot_general | solution.py:61
  78.0 0.5 fusion.13
  78.5 0.0 copy-done.3
  78.5 0.0 copy-start.5
  78.5 0.4 fusion.9
  78.9 0.1 copy-done.2
  79.1 0.7 pad_maximum_fusion
  79.8 3.4 %all-to-all-start.2 = ((bf16[8,2,8,768]{3,2,1,0:T(8,128)(2,1)}), bf16[8,2,8,768]{3,2,1,0:T(8,128)(2,1)S(1)}, u32[]{:S(2)}, u32[]{:S(2)}) async-start(bf16[8,2,8,768]{3,2,1,0:T(8,128)(2,1)} %bitcast.20), calls=%async_computation.2 | async-start | bytes 393216 | tf_op jit(solution)/shard_map/all_to_all | solution.py:105
  83.2 6.2 %all-to-all-done.2 = bf16[8,2,8,768]{3,2,1,0:T(8,128)(2,1)S(1)} async-done(((bf16[8,2,8,768]{3,2,1,0:T(8,128)(2,1)}), bf16[8,2,8,768]{3,2,1,0:T(8,128)(2,1)S(1)}, u32[]{:S(2)}, u32[]{:S(2)}) %all-to-all-start.2) | async-done | bytes 196640 | tf_op jit(solution)/shard_map/all_to_all | solution.py:105
  89.6 1.3 add_convert_fusion
  90.8 13.4 %all-to-all-start.3 = ((bf16[64,8,768]{2,1,0:T(8,128)(2,1)}), bf16[64,8,768]{2,1,0:T(8,128)(2,1)S(1)}, u32[]{:S(2)}, u32[]{:S(2)}) async-start(bf16[64,8,768]{2,1,0:T(8,128)(2,1)} %add_convert_fusion), calls=%async_computation.3 | async-start | bytes 1572864 | tf_op jit(solution)/shard_map/all_to_all | solution.py:120
  104.2 0.2 rev.3
  104.6 23.9 %all-to-all-done.3 = bf16[64,8,768]{2,1,0:T(8,128)(2,1)S(1)} async-done(((bf16[64,8,768]{2,1,0:T(8,128)(2,1)}), bf16[64,8,768]{2,1,0:T(8,128)(2,1)S(1)}, u32[]{:S(2)}, u32[]{:S(2)}) %all-to-all-start.3) | async-done | bytes 786464 | tf_op jit(solution)/shard_map/all_to_all | solution.py:120
  128.5 0.1 convert_reduce_fusion
  128.6 0.7 fusion.24
  (39 shorter events, 0.3 us)
Async XLA Ops:
  7.2 59.6 %copy-start = (bf16[3,192,768]{2,1,0:T(8,128)(2,1)S(1)}, bf16[3,192,768]{2,1,0:T(8,128)(2,1)}, u32[]{:S(2)}) copy-start(bf16[3,192,768]{2,1,0:T(8,128)(2,1)} %param.13) | copy-start | bytes 2654212
  7.2 19.0 %copy-start.10 = (s32[3,1]{0,1:T(1,128)S(1)}, s32[3,1]{0,1:T(1,128)}, u32[]{:S(2)}) copy-start(s32[3,1]{0,1:T(1,128)} %param.10) | copy-start | bytes 40
  7.2 21.5 %copy-start.9 = (s32[3]{0:T(128)S(1)}, s32[3]{0:T(128)}, u32[]{:S(2)}) copy-start(s32[3]{0:T(128)} %param.9) | copy-start | bytes 40
  7.2 66.5 %all-gather.2.cloned.1.call-start = ((), (), s32[]{:S(2)}) async-start(), calls=%async_computation.4 | async-start | bytes 5898240 | tf_op jit(solution)/shard_map/all_gather | solution.py:58
  9.6 40.6 %all-to-all-start = ((bf16[64,8,768]{2,1,0:T(8,128)(2,1)}), bf16[64,8,768]{2,1,0:T(8,128)(2,1)S(1)}, u32[]{:S(2)}, u32[]{:S(2)}) async-start(bf16[64,8,768]{2,1,0:T(8,128)(2,1)} %broadcast_in_dim.101), calls=%async_computation | async-start | bytes 1572864 | tf_op jit(solution)/shard_map/all_to_all | solution.py:14
  26.8 3.1 %collective-permute-start = (s32[1]{0:T(128)}, s32[1]{0:T(128)}, u32[]{:S(2)}, u32[]{:S(2)}) collective-permute-start(s32[1]{0:T(128)} %bitcast.3), channel_id=1, source_target_pairs={{0,4},{4,0},{1,5},{5,1},{2,6},{6,2},{3,7},{7,3},{8,12},{12,8},{9,1... | collective-permute-start | bytes 20 | tf_op jit(solution)/shard_map/ppermute | solution.py:69
  50.1 4.6 %collective-permute-start.1 = (bf16[8,768]{1,0:T(8,128)(2,1)S(1)}, bf16[8,768]{1,0:T(8,128)(2,1)S(1)}, u32[]{:S(2)}, u32[]{:S(2)}) collective-permute-start(bf16[8,768]{1,0:T(8,128)(2,1)S(1)} %get-tuple-element.4), channel_id=1, source_target_pairs={{0,4},{4,0},{1,5},{5,1},{2,6},{6,2},{3,7},{7,3},{8,12},{12,8},{9,1... | collective-permute-start | bytes 36872 | tf_op jit(solution)/shard_map/ppermute | solution.py:71
  55.4 11.4 %all-to-all-start.1 = ((bf16[4,2,8,768]{3,2,1,0:T(8,128)(2,1)}), bf16[4,2,8,768]{3,2,1,0:T(8,128)(2,1)S(1)}, u32[]{:S(2)}, u32[]{:S(2)}) async-start(bf16[4,2,8,768]{3,2,1,0:T(8,128)(2,1)} %broadcast_in_dim.102), calls=%async_computation.1 | async-start | bytes 196608 | tf_op jit(solution)/shard_map/all_to_all | solution.py:14
  67.9 10.6 %copy-start.1 = (bf16[3,256,768]{2,1,0:T(8,128)(2,1)S(1)}, bf16[3,256,768]{2,1,0:T(8,128)(2,1)}, u32[]{:S(2)}) copy-start(bf16[3,256,768]{2,1,0:T(8,128)(2,1)} %param.12) | copy-start | bytes 3538948
  73.7 4.8 %copy-start.3 = (f32[3,32,768]{2,1,0:T(8,128)S(1)}, f32[3,32,768]{2,1,0:T(8,128)}, u32[]{:S(2)}) copy-start(f32[3,32,768]{2,1,0:T(8,128)} %fusion.20) | copy-start | bytes 884740
  78.0 1.0 copy-start.2
  78.5 1.3 copy-start.5
  79.8 9.7 %all-to-all-start.2 = ((bf16[8,2,8,768]{3,2,1,0:T(8,128)(2,1)}), bf16[8,2,8,768]{3,2,1,0:T(8,128)(2,1)S(1)}, u32[]{:S(2)}, u32[]{:S(2)}) async-start(bf16[8,2,8,768]{3,2,1,0:T(8,128)(2,1)} %bitcast.20), calls=%async_computation.2 | async-start | bytes 393216 | tf_op jit(solution)/shard_map/all_to_all | solution.py:105
  83.2 21.0 %copy-start.4 = (bf16[1,8,768]{2,1,0:T(8,128)(2,1)S(1)}, bf16[1,8,768]{2,1,0:T(8,128)(2,1)}, u32[]{:S(2)}) copy-start(bf16[1,8,768]{2,1,0:T(8,128)(2,1)} %param.14) | copy-start | bytes 36868
  89.5 15.0 %copy-start.7 = (f32[1,768]{1,0:T(1,128)S(1)}, f32[1,768]{1,0:T(1,128)}, u32[]{:S(2)}) copy-start(f32[1,768]{1,0:T(1,128)} %param.17) | copy-start | bytes 9220
  89.5 15.0 %copy-start.8 = (f32[1,768]{1,0:T(1,128)S(1)}, f32[1,768]{1,0:T(1,128)}, u32[]{:S(2)}) copy-start(f32[1,768]{1,0:T(1,128)} %param.16) | copy-start | bytes 9220
  89.6 39.0 %copy-start.6 = (f32[1,8,768]{2,1,0:T(8,128)S(1)}, f32[1,8,768]{2,1,0:T(8,128)}, u32[]{:S(2)}) copy-start(f32[1,8,768]{2,1,0:T(8,128)} %param.15) | copy-start | bytes 73732
  90.8 37.6 %all-to-all-start.3 = ((bf16[64,8,768]{2,1,0:T(8,128)(2,1)}), bf16[64,8,768]{2,1,0:T(8,128)(2,1)S(1)}, u32[]{:S(2)}, u32[]{:S(2)}) async-start(bf16[64,8,768]{2,1,0:T(8,128)(2,1)} %add_convert_fusion), calls=%async_computation.3 | async-start | bytes 1572864 | tf_op jit(solution)/shard_map/all_to_all | solution.py:120
Sparse Core Ops, SparseCore 0:
  10.1 63.5 all-gather.1
where the time goes:
time: 137 us; the launch traced here: 136 us
  waiting for transfers between devices  62.5 us (46%)
  starting transfers between devices  41.5 us (30%)
  between operations  19.6 us (14%)
  matrix products  6.18 us (5%)
  local copies, waits for them, and re-layouts  3.31 us (2%)
  other arithmetic  3.12 us (2%)
    all_to_all x2, waiting for transfers between devices, copy_for_each(): lax.all_to_all(jnp.broadcast_to(x[None], (length, *x.shape)), axis, 0, 0,...  24.7 us
    all_to_all x1, waiting for transfers between devices, body(): lax.all_to_all(dense.astype(jnp.bfloat16), PLANE, split_axis=0, concat_ax...  23.9 us
    all_to_all x2, starting transfers between devices, copy_for_each(): lax.all_to_all(jnp.broadcast_to(x[None], (length, *x.shape)), axis, 0, 0,...  20.9 us
    all_to_all x1, starting transfers between devices, body(): lax.all_to_all(dense.astype(jnp.bfloat16), PLANE, split_axis=0, concat_ax...  13.4 us
    all_to_all x1, waiting for transfers between devices, body(): lax.all_to_all(send.reshape(2 * nharm, 2, rows_q, width).astype(jnp.bfloa...  6.23 us
    all_gather x1, waiting for transfers between devices, body(): piece = lax.all_gather(coupling, 'harm', axis=1, tiled=True)  5.86 us
    dot_general x1, matrix products, body(): jnp.einsum('sfg,sgn->sfn', front_live, piece, preferred_element_type=jnp....  4.24 us
    all_to_all x1, starting transfers between devices, body(): lax.all_to_all(send.reshape(2 * nharm, 2, rows_q, width).astype(jnp.bfloa...  3.42 us
  transfers between devices with their start and end apart: 7, of which 6 were waited for; matrix products, arithmetic and copies ran while one was open for 3% of the time, Pallas kernels for 0%

commit v1 on v0

--- a/solution.py
+++ b/solution.py
@@ -7,6 +7,11 @@
 SUB = ("sub_0", "sub_1", "sub_2")
 PLANE = ("sub_0", "sub_1")
 PAIR = ("sub_2", "harm")
+
+
+def gather_from_all(x, axis, dim):
+    copies = jnp.concatenate([x] * lax.axis_size(axis), axis=dim)
+    return lax.all_to_all(copies, axis, dim, dim, tiled=True)
 
 
 def copy_for_each(x, axis):
@@ -55,7 +60,7 @@
     own_rows = harm_idx * front_q + jnp.arange(front_q, dtype=jnp.int32)
     live_rows = own_rows[None, :] < lengths[:, None]
     masked = jnp.where(live_rows[:, :, None], coupling, jnp.zeros_like(coupling))
-    piece = lax.all_gather(coupling, "harm", axis=1, tiled=True)
+    piece = gather_from_all(coupling, "harm", 1)
     live_cols = jnp.arange(nharm * front_q, dtype=jnp.int32)[None, :] < lengths[:, None]
     front_live = jnp.where(live_cols[:, None, :], front_inverse, jnp.zeros_like(front_inverse))
     modes = jnp.einsum(

time: 137 us -> 188 us (1.37)
  waiting for transfers between devices: 62.5 us -> 120 us
  between operations: 19.6 us -> 6.45 us
  other arithmetic: 3.12 us -> 9.46 us
  local copies, waits for them, and re-layouts: 3.31 us -> 5.68 us
    all_to_all x0 -> x1, waiting for transfers between devices: none -> 71.4 us  [gather_from_all(): return lax.all_to_all(copies, axis, dim, dim, tiled=True)]
    all_to_all x2, waiting for transfers between devices: 24.7 us -> 17.5 us  [copy_for_each(): lax.all_to_all(jnp.broadcast_to(x[None], (length, *x.shape)), axis, 0, 0,...]
    all_to_all x1, starting transfers between devices: 13.4 us -> 6.55 us  [body(): lax.all_to_all(dense.astype(jnp.bfloat16), PLANE, split_axis=0, concat_ax...]
    concatenate x0 -> x1, other arithmetic: none -> 6.33 us  [gather_from_all(): copies = jnp.concatenate([x] * lax.axis_size(axis), axis=dim)]
    all_gather x1 -> x0, waiting for transfers between devices: 5.86 us -> none  [body(): piece = lax.all_gather(coupling, 'harm', axis=1, tiled=True)]
    all_to_all x0 -> x1, starting transfers between devices: none -> 5.4 us  [gather_from_all(): return lax.all_to_all(copies, axis, dim, dim, tiled=True)]
    unnamed x22 -> x21, local copies, waits for them, and re-layouts: 0.16 us -> 2.45 us
  transfers between devices with their start and end apart: 7 -> 7, of which waited for: 6 -> 5; matrix products, arithmetic and copies ran while one was open for 3% -> 5% of each run, Pallas kernels for 0% -> 0%
where the time goes in v1:
time: 188 us
  waiting for transfers between devices  120 us (64%)
  starting transfers between devices  40 us (21%)
  other arithmetic  9.46 us (5%)
  between operations  6.45 us (3%)
  matrix products  5.91 us (3%)
  local copies, waits for them, and re-layouts  5.68 us (3%)
    all_to_all x1, waiting for transfers between devices, gather_from_all(): return lax.all_to_all(copies, axis, dim, dim, tiled=True)  71.4 us
    all_to_all x1, waiting for transfers between devices, body(): lax.all_to_all(dense.astype(jnp.bfloat16), PLANE, split_axis=0, concat_ax...  23.9 us
    all_to_all x2, starting transfers between devices, copy_for_each(): lax.all_to_all(jnp.broadcast_to(x[None], (length, *x.shape)), axis, 0, 0,...  20.9 us
    all_to_all x2, waiting for transfers between devices, copy_for_each(): lax.all_to_all(jnp.broadcast_to(x[None], (length, *x.shape)), axis, 0, 0,...  17.5 us
    all_to_all x1, starting transfers between devices, body(): lax.all_to_all(dense.astype(jnp.bfloat16), PLANE, split_axis=0, concat_ax...  6.55 us
    concatenate x1, other arithmetic, gather_from_all(): copies = jnp.concatenate([x] * lax.axis_size(axis), axis=dim)  6.33 us
    all_to_all x1, waiting for transfers between devices, body(): lax.all_to_all(send.reshape(2 * nharm, 2, rows_q, width).astype(jnp.bfloa...  6.15 us
    all_to_all x1, starting transfers between devices, gather_from_all(): return lax.all_to_all(copies, axis, dim, dim, tiled=True)  5.4 us
  transfers between devices with their start and end apart: 7, of which 5 were waited for; matrix products, arithmetic and copies ran while one was open for 5% of the time, Pallas kernels for 0%

profile of v1, /device:TPU:8, one launch (start us, length us, event | category | flops | bytes accessed | tf_op | source)
XLA Modules:
  0.0 187.6 jit_solution(662922883978646098)
XLA Ops:
  0.6 0.0 copy-start
  0.7 1.7 broadcast_in_dim.101
  2.4 16.6 %all-to-all-start = ((bf16[64,8,768]{2,1,0:T(8,128)(2,1)}), bf16[64,8,768]{2,1,0:T(8,128)(2,1)S(1)}, u32[]{:S(2)}, u32[]{:S(2)}) async-start(bf16[64,8,768]{2,1,0:T(8,128)(2,1)} %broadcast_in_dim.101), calls=%async_computation | async-start | bytes 1572864 | tf_op jit(solution)/shard_map/all_to_all | solution.py:19
  19.0 0.6 slice.46
  19.6 1.9 %collective-permute-start = (s32[1]{0:T(128)}, s32[1]{0:T(128)}, u32[]{:S(2)}, u32[]{:S(2)}) collective-permute-start(s32[1]{0:T(128)} %bitcast.3), channel_id=1, source_target_pairs={{0,4},{4,0},{1,5},{5,1},{2,6},{6,2},{3,7},{7,3},{8,12},{12,8},{9,1... | collective-permute-start | bytes 20 | tf_op jit(solution)/shard_map/ppermute | solution.py:74
  21.5 1.2 collective-permute-done
  25.5 17.5 %all-to-all-done = bf16[64,8,768]{2,1,0:T(8,128)(2,1)S(1)} async-done(((bf16[64,8,768]{2,1,0:T(8,128)(2,1)}), bf16[64,8,768]{2,1,0:T(8,128)(2,1)S(1)}, u32[]{:S(2)}, u32[]{:S(2)}) %all-to-all-start) | async-done | bytes 786464 | tf_op jit(solution)/shard_map/all_to_all | solution.py:19
  42.9 1.9 %collective-permute-start.1 = (bf16[8,768]{1,0:T(8,128)(2,1)S(1)}, bf16[8,768]{1,0:T(8,128)(2,1)S(1)}, u32[]{:S(2)}, u32[]{:S(2)}) collective-permute-start(bf16[8,768]{1,0:T(8,128)(2,1)S(1)} %get-tuple-element.4), channel_id=1, source_target_pairs={{0,4},{4,0},{1,5},{5,1},{2,6},{6,2},{3,7},{7,3},{8,12},{12,8},{9,1... | collective-permute-start | bytes 36872 | tf_op jit(solution)/shard_map/ppermute | solution.py:76
  47.5 2.3 %copy.25 = bf16[3,256,768]{2,0,1:T(4,128)(2,1)S(1)} copy(bf16[3,256,768]{2,1,0:T(8,128)(2,1)} %param.12) | data formatting | bytes 2359296 | tf_op args[3]
  49.8 0.6 broadcast_in_dim.102
  50.5 4.3 %all-to-all-start.1 = ((bf16[4,2,8,768]{3,2,1,0:T(8,128)(2,1)}), bf16[4,2,8,768]{3,2,1,0:T(8,128)(2,1)S(1)}, u32[]{:S(2)}, u32[]{:S(2)}) async-start(bf16[4,2,8,768]{3,2,1,0:T(8,128)(2,1)} %broadcast_in_dim.102), calls=%async_computation.1 | async-start | bytes 196608 | tf_op jit(solution)/shard_map/all_to_all | solution.py:19
  54.8 6.3 %pad_maximum_fusion = bf16[3,1024,768]{2,0,1:T(4,128)(2,1)} fusion(bf16[3,256,768]{2,0,1:T(4,128)(2,1)S(1)} %copy.25), kind=kLoop, calls=%fused_computation | loop fusion | flops 7077888 | bytes 5898240 | tf_op jit(solution)/shard_map/concatenate | solution.py:13
  61.1 5.4 %all-to-all-start.2 = ((bf16[3,1024,768]{2,0,1:T(4,128)(2,1)}), bf16[3,1024,768]{2,0,1:T(4,128)(2,1)}, u32[]{:S(2)}, u32[]{:S(2)}) async-start(bf16[3,1024,768]{2,0,1:T(4,128)(2,1)} %pad_maximum_fusion), calls=%async_computation.2 | async-start | bytes 12582912 | tf_op jit(solution)/shard_map/all_to_all | solution.py:14
  66.5 0.1 broadcast_compare_fusion
  66.6 0.1 iota_compare_fusion
  66.7 0.3 fusion.23
  67.1 71.4 %all-to-all-done.2 = bf16[3,1024,768]{2,0,1:T(4,128)(2,1)} async-done(((bf16[3,1024,768]{2,0,1:T(4,128)(2,1)}), bf16[3,1024,768]{2,0,1:T(4,128)(2,1)}, u32[]{:S(2)}, u32[]{:S(2)}) %all-to-all-start.2) | async-done | bytes 4718624 | tf_op jit(solution)/shard_map/all_to_all | solution.py:14
  138.5 4.7 %fusion.4 = bf16[3,256,768]{2,1,0:T(8,128)(2,1)S(1)} fusion(bf16[3,1024,768]{2,0,1:T(4,128)(2,1)} %all-to-all-done.2, bf16[3,256,1024]{2,1,0:T(8,128)(2,1)} %param.11, pred[3,1024]{1,0:T(4,128)(4,1)S(1)} %iota_compare_fusion), kind=kOutput, calls=%fused_computation.7 | convolution fusion | flops 1209335808 | bytes 7474176 | tf_op jit(solution)/shard_map/sfg,sgn->sfn/dot_general | solution.py:66
  143.2 0.0 copy-start.1
  143.2 0.5 fusion.16
  143.7 0.0 copy-start.4
  143.7 0.4 fusion.12
  144.1 0.1 copy-done.1
  144.3 0.7 pad_maximum_fusion.1
  145.0 3.4 %all-to-all-start.3 = ((bf16[8,2,8,768]{3,2,1,0:T(8,128)(2,1)}), bf16[8,2,8,768]{3,2,1,0:T(8,128)(2,1)S(1)}, u32[]{:S(2)}, u32[]{:S(2)}) async-start(bf16[8,2,8,768]{3,2,1,0:T(8,128)(2,1)} %bitcast.20), calls=%async_computation.3 | async-start | bytes 393216 | tf_op jit(solution)/shard_map/all_to_all | solution.py:110
  148.4 6.1 %all-to-all-done.3 = bf16[8,2,8,768]{3,2,1,0:T(8,128)(2,1)S(1)} async-done(((bf16[8,2,8,768]{3,2,1,0:T(8,128)(2,1)}), bf16[8,2,8,768]{3,2,1,0:T(8,128)(2,1)S(1)}, u32[]{:S(2)}, u32[]{:S(2)}) %all-to-all-start.3) | async-done | bytes 196640 | tf_op jit(solution)/shard_map/all_to_all | solution.py:110
  154.7 1.3 add_convert_fusion
  155.9 6.6 %all-to-all-start.4 = ((bf16[64,8,768]{2,1,0:T(8,128)(2,1)}), bf16[64,8,768]{2,1,0:T(8,128)(2,1)S(1)}, u32[]{:S(2)}, u32[]{:S(2)}) async-start(bf16[64,8,768]{2,1,0:T(8,128)(2,1)} %add_convert_fusion), calls=%async_computation.4 | async-start | bytes 1572864 | tf_op jit(solution)/shard_map/all_to_all | solution.py:125
  162.5 0.2 rev.3
  162.9 23.9 %all-to-all-done.4 = bf16[64,8,768]{2,1,0:T(8,128)(2,1)S(1)} async-done(((bf16[64,8,768]{2,1,0:T(8,128)(2,1)}), bf16[64,8,768]{2,1,0:T(8,128)(2,1)S(1)}, u32[]{:S(2)}, u32[]{:S(2)}) %all-to-all-start.4) | async-done | bytes 786464 | tf_op jit(solution)/shard_map/all_to_all | solution.py:125
  186.8 0.1 convert_reduce_fusion
  186.9 0.7 fusion.27
  (38 shorter events, 0.3 us)
Async XLA Ops:
  0.6 66.1 %copy-start = (bf16[3,192,768]{2,1,0:T(8,128)(2,1)S(1)}, bf16[3,192,768]{2,1,0:T(8,128)(2,1)}, u32[]{:S(2)}) copy-start(bf16[3,192,768]{2,1,0:T(8,128)(2,1)} %param.13) | copy-start | bytes 2654212
  0.6 18.3 %copy-start.9 = (s32[3,1]{0,1:T(1,128)S(1)}, s32[3,1]{0,1:T(1,128)}, u32[]{:S(2)}) copy-start(s32[3,1]{0,1:T(1,128)} %param.10) | copy-start | bytes 40
  2.4 40.6 %all-to-all-start = ((bf16[64,8,768]{2,1,0:T(8,128)(2,1)}), bf16[64,8,768]{2,1,0:T(8,128)(2,1)S(1)}, u32[]{:S(2)}, u32[]{:S(2)}) async-start(bf16[64,8,768]{2,1,0:T(8,128)(2,1)} %broadcast_in_dim.101), calls=%async_computation | async-start | bytes 1572864 | tf_op jit(solution)/shard_map/all_to_all | solution.py:19
  19.6 3.1 %collective-permute-start = (s32[1]{0:T(128)}, s32[1]{0:T(128)}, u32[]{:S(2)}, u32[]{:S(2)}) collective-permute-start(s32[1]{0:T(128)} %bitcast.3), channel_id=1, source_target_pairs={{0,4},{4,0},{1,5},{5,1},{2,6},{6,2},{3,7},{7,3},{8,12},{12,8},{9,1... | collective-permute-start | bytes 20 | tf_op jit(solution)/shard_map/ppermute | solution.py:74
  42.9 6.8 %collective-permute-start.1 = (bf16[8,768]{1,0:T(8,128)(2,1)S(1)}, bf16[8,768]{1,0:T(8,128)(2,1)S(1)}, u32[]{:S(2)}, u32[]{:S(2)}) collective-permute-start(bf16[8,768]{1,0:T(8,128)(2,1)S(1)} %get-tuple-element.4), channel_id=1, source_target_pairs={{0,4},{4,0},{1,5},{5,1},{2,6},{6,2},{3,7},{7,3},{8,12},{12,8},{9,1... | collective-permute-start | bytes 36872 | tf_op jit(solution)/shard_map/ppermute | solution.py:76
  50.5 10.6 %all-to-all-start.1 = ((bf16[4,2,8,768]{3,2,1,0:T(8,128)(2,1)}), bf16[4,2,8,768]{3,2,1,0:T(8,128)(2,1)S(1)}, u32[]{:S(2)}, u32[]{:S(2)}) async-start(bf16[4,2,8,768]{3,2,1,0:T(8,128)(2,1)} %broadcast_in_dim.102), calls=%async_computation.1 | async-start | bytes 196608 | tf_op jit(solution)/shard_map/all_to_all | solution.py:19
  61.1 5.4 %copy-start.8 = (s32[3]{0:T(128)S(1)}, s32[3]{0:T(128)}, u32[]{:S(2)}) copy-start(s32[3]{0:T(128)} %param.9) | copy-start | bytes 40
  61.1 77.4 %all-to-all-start.2 = ((bf16[3,1024,768]{2,0,1:T(4,128)(2,1)}), bf16[3,1024,768]{2,0,1:T(4,128)(2,1)}, u32[]{:S(2)}, u32[]{:S(2)}) async-start(bf16[3,1024,768]{2,0,1:T(4,128)(2,1)} %pad_maximum_fusion), calls=%async_computation.2 | async-start | bytes 12582912 | tf_op jit(solution)/shard_map/all_to_all | solution.py:14
  67.1 76.6 %copy-start.2 = (bf16[3,256,768]{2,1,0:T(8,128)(2,1)S(1)}, bf16[3,256,768]{2,1,0:T(8,128)(2,1)}, u32[]{:S(2)}) copy-start(bf16[3,256,768]{2,1,0:T(8,128)(2,1)} %param.12) | copy-start | bytes 3538948
  143.2 1.0 copy-start.1
  143.7 1.3 copy-start.4
  145.0 9.6 %all-to-all-start.3 = ((bf16[8,2,8,768]{3,2,1,0:T(8,128)(2,1)}), bf16[8,2,8,768]{3,2,1,0:T(8,128)(2,1)S(1)}, u32[]{:S(2)}, u32[]{:S(2)}) async-start(bf16[8,2,8,768]{3,2,1,0:T(8,128)(2,1)} %bitcast.20), calls=%async_computation.3 | async-start | bytes 393216 | tf_op jit(solution)/shard_map/all_to_all | solution.py:110
  148.4 14.1 %copy-start.3 = (bf16[1,8,768]{2,1,0:T(8,128)(2,1)S(1)}, bf16[1,8,768]{2,1,0:T(8,128)(2,1)}, u32[]{:S(2)}) copy-start(bf16[1,8,768]{2,1,0:T(8,128)(2,1)} %param.14) | copy-start | bytes 36868
  154.6 8.2 %copy-start.6 = (f32[1,768]{1,0:T(1,128)S(1)}, f32[1,768]{1,0:T(1,128)}, u32[]{:S(2)}) copy-start(f32[1,768]{1,0:T(1,128)} %param.17) | copy-start | bytes 9220
  154.6 8.2 %copy-start.7 = (f32[1,768]{1,0:T(1,128)S(1)}, f32[1,768]{1,0:T(1,128)}, u32[]{:S(2)}) copy-start(f32[1,768]{1,0:T(1,128)} %param.16) | copy-start | bytes 9220
  154.7 32.2 %copy-start.5 = (f32[1,8,768]{2,1,0:T(8,128)S(1)}, f32[1,8,768]{2,1,0:T(8,128)}, u32[]{:S(2)}) copy-start(f32[1,8,768]{2,1,0:T(8,128)} %param.15) | copy-start | bytes 73732
  155.9 30.8 %all-to-all-start.4 = ((bf16[64,8,768]{2,1,0:T(8,128)(2,1)}), bf16[64,8,768]{2,1,0:T(8,128)(2,1)S(1)}, u32[]{:S(2)}, u32[]{:S(2)}) async-start(bf16[64,8,768]{2,1,0:T(8,128)(2,1)} %add_convert_fusion), calls=%async_computation.4 | async-start | bytes 1572864 | tf_op jit(solution)/shard_map/all_to_all | solution.py:125
